TPU v7x, 256 devices: a whole 4x4x8 slice. The times are simulated.
256 devices in a mesh: grp: 32 (over x, z), shard: 8 (over y, core).
Axes of the slice: x: 4, y: 4, z: 8, core: 2. Of those that a mesh axis runs over, the one named last changes fastest.
Arguments:
- layer_inputs: bfloat16 [131072, 1600], P(('grp', 'shard')), may hold values from -6 to 6
- cotangents: bfloat16 [131072, 1600], P(('grp', 'shard')), may hold values from -0.25 to 0.25
- weight: bfloat16 [1600, 1600], P('shard'), may hold values from -0.15625 to 0.15625
- error_state: float32 [32, 1600, 1600], P('grp', 'shard'), may hold values from -6 to 6
- momentum: float32 [1600, 1600], P('shard'), may hold values from -0.75 to 0.75
- bias_momentum: float32 [1600], replicated, may hold values from -6 to 6
- start_basis: float32 [1600, 32], replicated, may hold values from -6 to 6
- next_inputs: bfloat16 [131072, 1600], P(('grp', 'shard')), may hold values from -6 to 6
Outputs:
- next_outputs: bfloat16 [131072, 1600], P(('grp', 'shard'))
- new_error: float32 [32, 1600, 1600], P('grp', 'shard')
- new_momentum: float32 [1600, 1600], P('shard')
- new_bias_momentum: float32 [1600], replicated
All inputs are finite; a program needn't handle non-finite values.
Results may differ from a plain program's by a relative error of at most 0.015.
Values may be sent and summed in bfloat16 or wider, within the bound.
No kernel may reach another device: no remote copies, remote signals or barrier semaphores. Data moves between devices by JAX's collectives and lax.ppermute only.
A program may use at most 128 MiB of HBM per device.

v0:
```python
import jax
import jax.numpy as jnp
from jax import lax
from jax.sharding import PartitionSpec as P

momentum_decay = 0.9
learn_rate = 0.1


def shards(
    layer_inputs, cotangents, weight, error_state, momentum, bias_momentum, start_basis, next_inputs
):
    highest = lax.Precision.HIGHEST
    group_count = lax.axis_size("grp")
    rank = start_basis.shape[1]
    gradient = lax.psum_scatter(
        lax.dot_general(
            layer_inputs, cotangents, (((0,), (0,)), ((), ())), preferred_element_type=jnp.float32
        ).astype(jnp.bfloat16),
        "shard",
        scatter_dimension=0,
        tiled=True,
    ).astype(jnp.float32)
    column_sums = jnp.sum(cotangents, axis=0, dtype=jnp.float32)
    corrected = gradient + error_state[0]
    summed = lax.psum(jnp.concatenate([corrected, column_sums[None, :]], axis=0), "grp")
    total = summed[:-1]
    grp_sums = summed[-1]
    basis = start_basis
    ortho = start_basis
    for round_index in range(2):
        factor = jnp.dot(total, basis, precision=highest)
        gram_part = jnp.dot(factor.T, factor, precision=highest)
        if round_index == 0:
            packed = lax.psum(jnp.concatenate([gram_part.reshape(-1), grp_sums]), "shard")
            gram = packed[: rank * rank].reshape(rank, rank)
            all_sums = packed[rank * rank :]
        else:
            gram = lax.psum(gram_part, "shard")
        lower_factor = jnp.linalg.cholesky(gram)
        ortho = jax.scipy.linalg.solve_triangular(lower_factor, factor.T, lower=True).T
        partial_basis = lax.dot_general(total, ortho, (((0,), (0,)), ((), ())), precision=highest)
        basis = lax.psum(partial_basis, "shard") / group_count
    approx = jnp.dot(ortho, basis.T, precision=highest)
    new_error = (corrected - approx)[None, :, :]
    new_momentum = momentum_decay * momentum + approx
    new_bias_momentum = momentum_decay * bias_momentum + all_sums / group_count
    new_weight = (weight.astype(jnp.float32) - learn_rate * new_momentum).astype(jnp.bfloat16)
    projected = jnp.dot(
        next_inputs,
        lax.all_gather(new_weight, "shard", axis=0, tiled=True),
        preferred_element_type=jnp.float32,
    )
    return (projected.astype(jnp.bfloat16), new_error, new_momentum, new_bias_momentum)


def solution(mesh):
    placed = (
        P(("grp", "shard"), None),
        P(("grp", "shard"), None),
        P("shard", None),
        P("grp", "shard", None),
        P("shard", None),
        P(),
        P(),
        P(("grp", "shard"), None),
    )
    return jax.shard_map(
        shards,
        mesh=mesh,
        in_specs=placed,
        out_specs=(P(("grp", "shard"), None), P("grp", "shard", None), P("shard", None), P()),
        check_vma=False,
    )
```

profile of v0, /device:TPU:1, one launch (start us, length us, event | category | flops | bytes accessed | tf_op | source)
XLA Modules:
  0.0 473.4 jit_solution(3598170805652788617)
XLA Ops:
  7.2 0.0 copy-start
  7.2 0.0 reduce-scatter.4.cloned.1.call-start
  7.2 1.4 copy-done
  8.6 6.3 %convolution_convert_fusion = bf16[1600,1600]{1,0:T(8,128)(2,1)} fusion(bf16[512,1600]{0,1:T(8,128)(2,1)S(1)} %copy-done, bf16[512,1600]{0,1:T(8,128)(2,1)} %param.12), kind=kOutput, calls=%fused_computation | convolution fusion | flops 2624000000 | bytes 8396800 | tf_op jit(solution)/shard_map/dot_general | solution.py:17
  14.9 0.0 copy-start.3
  14.9 0.0 reduce-scatter.4.cloned.1.call-update
  14.9 0.0 all-reduce.5.cloned.1.call-start
  15.0 1.4 copy-done.3
  16.4 0.3 convert_reduce_fusion
  16.7 48.7 %reduce-scatter.4.cloned.1.call-done = bf16[200,1600]{1,0:T(8,128)(2,1)} async-done(((bf16[1600,1600]{1,0:T(8,128)(2,1)}), bf16[200,1600]{1,0:T(8,128)(2,1)}) %reduce-scatter.4.cloned.1.call-update) | async-done | bytes 640016
  65.4 1.6 bitcast_add_fusion
  67.0 0.0 copy-start.2
  67.0 1.1 copy-done.2
  68.1 0.0 copy-start.4
  68.1 1.2 pad_maximum_fusion
  69.3 0.0 all-reduce.5.cloned.1.call-update
  69.3 0.0 all-reduce.7.cloned.1.call-start
  69.3 149.4 %all-reduce.5.cloned.1.call-done = f32[201,1600]{1,0:T(8,128)} async-done(((f32[201,1600]{1,0:T(8,128)}), f32[201,1600]{1,0:T(8,128)}) %all-reduce.5.cloned.1.call-update) | async-done | bytes 1286416 | tf_op jit(solution)/shard_map/psum | solution.py:26
  218.7 0.0 copy-done.4
  218.7 0.0 copy-start.1
  218.7 2.8 fusion.7
  221.5 0.2 fusion.31
  221.7 0.1 reshape.30
  221.7 0.0 copy-done.1
  221.8 25.7 %psum.36 = f32[2624]{0:T(1024)S(1)} all-reduce(f32[2624]{0:T(1024)S(1)} %pad_maximum_fusion.1), channel_id=1, replica_groups=mesh['grp'=32,'shard'=8] {'shard'}, use_global_device_ids=true, to_apply=%region_3.0 | all-reduce | flops 2624 | bytes 20992 | tf_op jit(solution)/shard_map/psum | solution.py:35
  247.5 0.1 reshape.31
  247.6 0.1 copy.18
  247.7 2.9 cholesky.44
  250.6 0.6 compare_reduce_fusion.1
  251.3 0.7 fusion.18
  251.9 2.4 custom-call.6
  254.4 0.2 fusion.16
  254.6 1.7 fusion.5
  256.3 0.0 all-reduce.7.cloned.1.call-update
  256.3 0.0 all-reduce.9.cloned.1.call-start
  256.4 60.6 %all-reduce.7.cloned.1.call-done = f32[1600,32]{0,1:T(8,128)} async-done(((f32[1600,32]{0,1:T(8,128)}), f32[1600,32]{0,1:T(8,128)}) %all-reduce.7.cloned.1.call-update) | async-done | bytes 204816 | tf_op jit(solution)/shard_map/psum | solution.py:43
  317.0 2.3 fusion.3
  319.2 0.2 fusion.32
  319.4 21.9 %psum.38 = f32[32,32]{0,1:T(8,128)S(1)} all-reduce(f32[32,32]{0,1:T(8,128)S(1)} %fusion.32), channel_id=1, replica_groups=mesh['grp'=32,'shard'=8] {'shard'}, use_global_device_ids=true, to_apply=%region_7.10 | all-reduce | flops 1024 | bytes 8192 | tf_op jit(solution)/shard_map/psum | solution.py:39
  341.3 0.1 copy.20
  341.4 2.9 cholesky.55
  344.4 0.6 compare_reduce_fusion
  345.0 0.7 fusion.19
  345.7 2.4 custom-call.7
  348.1 0.2 fusion.14
  348.3 1.7 fusion.1
  350.0 0.0 all-reduce.9.cloned.1.call-update
  350.0 0.0 copy-start.5
  350.0 0.0 all-gather.2.cloned.1.call-start
  350.1 64.9 %all-reduce.9.cloned.1.call-done = f32[1600,32]{0,1:T(8,128)} async-done(((f32[1600,32]{0,1:T(8,128)}), f32[1600,32]{0,1:T(8,128)}) %all-reduce.9.cloned.1.call-update) | async-done | bytes 204816 | tf_op jit(solution)/shard_map/psum | solution.py:43
  415.0 5.2 %subtract_convert_fusion = (bf16[200,1600]{1,0:T(8,128)(2,1)}, f32[200,1600]{1,0:T(8,128)}, f32[1,200,1600]{2,1,0:T(8,128)}) fusion(bf16[200,1600]{1,0:T(8,128)(2,1)} %param.13, f32[200,1600]{1,0:T(8,128)} %param.15, f32[200,1600]{1,0:T(8,128)} %copy-done.2, f32[32,200]{1,0:T(8,128)S(1)} %fusion.14, f32[1600,32]{0,1:T(8,128)} %all-reduce.9.cloned.1.call-done), kind=kOutput, calls=%fused_computation.7 | convolution fusion | flops 125171200 | bytes 6630400 | tf_op jit(solution)/shard_map/dot_general | solution.py:44
  420.2 0.0 all-gather.2.cloned.1.call-update
  420.2 0.0 copy-done.5
  420.2 0.6 fusion.26
  420.8 38.7 %all-gather.2.cloned.1.call-done = bf16[1600,1600]{1,0:T(8,128)(2,1)} async-done(((bf16[200,1600]{1,0:T(8,128)(2,1)}), bf16[1600,1600]{1,0:T(8,128)(2,1)}) %all-gather.2.cloned.1.call-update) | async-done | bytes 5120016 | tf_op jit(solution)/shard_map/all_gather | solution.py:51
  459.5 7.4 %fusion = bf16[512,1600]{0,1:T(8,128)(2,1)} fusion(bf16[1600,1600]{1,0:T(8,128)(2,1)} %all-gather.2.cloned.1.call-done, bf16[512,1600]{0,1:T(8,128)(2,1)} %param.18), kind=kOutput, calls=%fused_computation.3 | convolution fusion | flops 2622259200 | bytes 8396800 | tf_op jit(solution)/shard_map/dot_general | solution.py:49
  (8 shorter events, 0.1 us)
Async XLA Ops:
  7.2 1.4 copy-start
  7.2 58.2 %reduce-scatter.4.cloned.1.call-start = ((), (), s32[]{:S(2)}) async-start(), calls=%async_computation.5 | async-start | bytes 5990400
  14.9 1.4 copy-start.3
  14.9 203.7 %all-reduce.5.cloned.1.call-start = ((), (), s32[]{:S(2)}) async-start(), calls=%async_computation.1 | async-start | bytes 2768896 | tf_op jit(solution)/shard_map/psum | solution.py:26
  67.0 1.1 copy-start.2
  68.1 150.6 %copy-start.4 = (f32[1600,32]{0,1:T(8,128)S(1)}, f32[1600,32]{0,1:T(8,128)}, u32[]{:S(2)}) copy-start(f32[1600,32]{0,1:T(8,128)} %param.17) | copy-start | bytes 614404
  69.3 247.7 %all-reduce.7.cloned.1.call-start = ((), (), s32[]{:S(2)}) async-start(), calls=%async_computation.2 | async-start | bytes 425984 | tf_op jit(solution)/shard_map/psum | solution.py:43
  218.7 3.0 copy-start.1
  256.3 158.7 %all-reduce.9.cloned.1.call-start = ((), (), s32[]{:S(2)}) async-start(), calls=%async_computation.3 | async-start | bytes 425984 | tf_op jit(solution)/shard_map/psum | solution.py:43
  350.0 70.2 %copy-start.5 = (f32[1600]{0:T(1024)S(1)}, f32[1600]{0:T(1024)}, u32[]{:S(2)}) copy-start(f32[1600]{0:T(1024)} %param.16) | copy-start | bytes 19204
  350.0 109.5 %all-gather.2.cloned.1.call-start = ((), (), s32[]{:S(2)}) async-start(), calls=%async_computation.4 | async-start | bytes 5990400 | tf_op jit(solution)/shard_map/all_gather | solution.py:51
Sparse Core Ops, SparseCore 0:
  15.1 50.2 reduce-scatter.3
  69.4 149.1 all-reduce.4
  256.4 60.4 all-reduce.6
  350.1 64.7 all-reduce.8
  420.3 39.1 all-gather.1
where the time goes:
time: 474 us; the launch traced here: 473 us
  waiting for transfers between devices  362 us (76%)
  blocking collectives  47.7 us (10%)
  matrix products  28.1 us (6%)
  other arithmetic  17.1 us (4%)
  between operations  13.9 us (3%)
    psum x1, waiting for transfers between devices, shards(): lax.psum(jnp.concatenate([corrected, column_sums[None, :]], axis=0), 'grp')  149 us
    psum x2, waiting for transfers between devices, shards(): basis = lax.psum(partial_basis, 'shard') / group_count  125 us
    unnamed x6, waiting for transfers between devices  48.8 us
    all_gather x1, waiting for transfers between devices, shards(): lax.all_gather(new_weight, 'shard', axis=0, tiled=True)  38.7 us
    psum x1, blocking collectives, shards(): lax.psum(jnp.concatenate([gram_part.reshape(-1), grp_sums]), 'shard')  25.7 us
    psum x1, blocking collectives, shards(): gram = lax.psum(gram_part, 'shard')  21.9 us
  transfers between devices with their start and end apart: 5, of which 5 were waited for; matrix products, arithmetic and copies ran while one was open for 0% of the time, Pallas kernels for 0%

commit v1 on v0

--- a/solution.py
+++ b/solution.py
@@ -10,6 +10,18 @@
 def shards(
     layer_inputs, cotangents, weight, error_state, momentum, bias_momentum, start_basis, next_inputs
 ):
+
+    def cover_sheet(xin, chip_axis):
+        return jnp.concatenate(
+            lax.all_to_all(
+                jnp.stack([xin for _ in range(lax.axis_size(chip_axis))]),
+                axis_name=chip_axis,
+                split_axis=0,
+                concat_axis=0,
+            ),
+            axis=0,
+        )
+
     highest = lax.Precision.HIGHEST
     group_count = lax.axis_size("grp")
     rank = start_basis.shape[1]
@@ -47,9 +59,7 @@
     new_bias_momentum = momentum_decay * bias_momentum + all_sums / group_count
     new_weight = (weight.astype(jnp.float32) - learn_rate * new_momentum).astype(jnp.bfloat16)
     projected = jnp.dot(
-        next_inputs,
-        lax.all_gather(new_weight, "shard", axis=0, tiled=True),
-        preferred_element_type=jnp.float32,
+        next_inputs, cover_sheet(new_weight, "shard"), preferred_element_type=jnp.float32
     )
     return (projected.astype(jnp.bfloat16), new_error, new_momentum, new_bias_momentum)
 

time: 474 us -> 504 us (1.063)
  waiting for transfers between devices: 362 us -> 384 us
  starting transfers between devices: 0.21 us -> 6.17 us
    all_to_all x0 -> x1, waiting for transfers between devices: none -> 60.3 us  [cover_sheet(): lax.all_to_all(jnp.stack([xin for _ in range(lax.axis_size(chip_axis))]),...]
    all_gather x1 -> x0, waiting for transfers between devices: 38.7 us -> none  [shards(): lax.all_gather(new_weight, 'shard', axis=0, tiled=True)]
    all_to_all x0 -> x1, starting transfers between devices: none -> 6 us  [cover_sheet(): lax.all_to_all(jnp.stack([xin for _ in range(lax.axis_size(chip_axis))]),...]
    unnamed x6 -> x5, waiting for transfers between devices: 48.8 us -> 48.7 us
where the time goes in v1:
time: 504 us; the launch traced here: 503 us
  waiting for transfers between devices  384 us (76%)
  blocking collectives  47.7 us (9%)
  matrix products  27.9 us (6%)
  other arithmetic  17.1 us (3%)
  between operations  13.9 us (3%)
  local copies, waits for them, and re-layouts  6.86 us (1%)
  starting transfers between devices  6.17 us (1%)
    psum x1, waiting for transfers between devices, shards(): lax.psum(jnp.concatenate([corrected, column_sums[None, :]], axis=0), 'grp')  149 us
    psum x2, waiting for transfers between devices, shards(): basis = lax.psum(partial_basis, 'shard') / group_count  126 us
    all_to_all x1, waiting for transfers between devices, cover_sheet(): lax.all_to_all(jnp.stack([xin for _ in range(lax.axis_size(chip_axis))]),...  60.3 us
    unnamed x5, waiting for transfers between devices  48.7 us
    psum x1, blocking collectives, shards(): lax.psum(jnp.concatenate([gram_part.reshape(-1), grp_sums]), 'shard')  25.7 us
    psum x1, blocking collectives, shards(): gram = lax.psum(gram_part, 'shard')  21.9 us
  transfers between devices with their start and end apart: 5, of which 5 were waited for; matrix products, arithmetic and copies ran while one was open for 0% of the time, Pallas kernels for 0%

profile of v1, /device:TPU:1, one launch (start us, length us, event | category | flops | bytes accessed | tf_op | source)
XLA Modules:
  0.0 503.2 jit_solution(12014447005722340320)
XLA Ops:
  7.2 0.0 copy-start
  7.2 0.0 reduce-scatter.4.cloned.1.call-start
  7.2 1.4 copy-done
  8.6 6.3 %convolution_convert_fusion = bf16[1600,1600]{1,0:T(8,128)(2,1)} fusion(bf16[512,1600]{0,1:T(8,128)(2,1)S(1)} %copy-done, bf16[512,1600]{0,1:T(8,128)(2,1)} %param.12), kind=kOutput, calls=%fused_computation | convolution fusion | flops 2624000000 | bytes 8396800 | tf_op jit(solution)/shard_map/dot_general | solution.py:29
  14.9 0.0 copy-start.3
  14.9 0.0 reduce-scatter.4.cloned.1.call-update
  15.0 0.0 all-reduce.5.cloned.1.call-start
  15.0 1.4 copy-done.3
  16.4 0.3 convert_reduce_fusion
  16.7 48.6 %reduce-scatter.4.cloned.1.call-done = bf16[200,1600]{1,0:T(8,128)(2,1)} async-done(((bf16[1600,1600]{1,0:T(8,128)(2,1)}), bf16[200,1600]{1,0:T(8,128)(2,1)}) %reduce-scatter.4.cloned.1.call-update) | async-done | bytes 640016
  65.3 1.6 bitcast_add_fusion
  66.9 0.0 copy-start.2
  66.9 1.1 copy-done.2
  68.0 0.0 copy-start.4
  68.0 1.2 pad_maximum_fusion
  69.1 0.0 all-reduce.5.cloned.1.call-update
  69.2 0.0 all-reduce.7.cloned.1.call-start
  69.2 149.1 %all-reduce.5.cloned.1.call-done = f32[201,1600]{1,0:T(8,128)} async-done(((f32[201,1600]{1,0:T(8,128)}), f32[201,1600]{1,0:T(8,128)}) %all-reduce.5.cloned.1.call-update) | async-done | bytes 1286416 | tf_op jit(solution)/shard_map/psum | solution.py:38
  218.4 0.0 copy-done.4
  218.4 0.0 copy-start.1
  218.4 2.8 fusion.7
  221.2 0.2 fusion.31
  221.3 0.1 reshape.35
  221.4 0.0 copy-done.1
  221.4 25.7 %psum.36 = f32[2624]{0:T(1024)S(1)} all-reduce(f32[2624]{0:T(1024)S(1)} %pad_maximum_fusion.1), channel_id=1, replica_groups=mesh['grp'=32,'shard'=8] {'shard'}, use_global_device_ids=true, to_apply=%region_3.0 | all-reduce | flops 2624 | bytes 20992 | tf_op jit(solution)/shard_map/psum | solution.py:47
  247.2 0.1 reshape.36
  247.3 0.1 copy.18
  247.3 2.9 cholesky.44
  250.3 0.6 compare_reduce_fusion.1
  250.9 0.7 fusion.18
  251.6 2.4 custom-call.6
  254.0 0.2 fusion.16
  254.3 1.7 fusion.5
  256.0 0.0 all-reduce.7.cloned.1.call-update
  256.0 0.0 all-reduce.9.cloned.1.call-start
  256.0 60.6 %all-reduce.7.cloned.1.call-done = f32[1600,32]{0,1:T(8,128)} async-done(((f32[1600,32]{0,1:T(8,128)}), f32[1600,32]{0,1:T(8,128)}) %all-reduce.7.cloned.1.call-update) | async-done | bytes 204816 | tf_op jit(solution)/shard_map/psum | solution.py:55
  316.6 2.3 fusion.3
  318.9 0.2 fusion.32
  319.1 21.9 %psum.38 = f32[32,32]{0,1:T(8,128)S(1)} all-reduce(f32[32,32]{0,1:T(8,128)S(1)} %fusion.32), channel_id=1, replica_groups=mesh['grp'=32,'shard'=8] {'shard'}, use_global_device_ids=true, to_apply=%region_7.10 | all-reduce | flops 1024 | bytes 8192 | tf_op jit(solution)/shard_map/psum | solution.py:51
  341.0 0.1 copy.20
  341.1 2.9 cholesky.55
  344.0 0.6 compare_reduce_fusion
  344.7 0.7 fusion.19
  345.3 2.4 custom-call.7
  347.8 0.2 fusion.14
  348.0 1.7 fusion.1
  349.7 0.0 all-reduce.9.cloned.1.call-update
  349.7 65.0 %all-reduce.9.cloned.1.call-done = f32[1600,32]{0,1:T(8,128)} async-done(((f32[1600,32]{0,1:T(8,128)}), f32[1600,32]{0,1:T(8,128)}) %all-reduce.9.cloned.1.call-update) | async-done | bytes 204816 | tf_op jit(solution)/shard_map/psum | solution.py:55
  414.6 5.0 subtract_convert_fusion
  419.6 2.7 stack.2
  422.3 0.0 copy-start.5
  422.3 6.0 %all-to-all-start = ((bf16[8,200,1600]{2,1,0:T(8,128)(2,1)}), bf16[8,200,1600]{2,1,0:T(8,128)(2,1)}, u32[]{:S(2)}, u32[]{:S(2)}) async-start(bf16[8,200,1600]{2,1,0:T(8,128)(2,1)} %stack.2), calls=%async_computation | async-start | bytes 10649600 | tf_op jit(solution)/shard_map/all_to_all | solution.py:16
  428.4 0.0 copy-done.5
  428.4 0.6 fusion.26
  429.0 60.3 %all-to-all-done = bf16[8,200,1600]{2,1,0:T(8,128)(2,1)} async-done(((bf16[8,200,1600]{2,1,0:T(8,128)(2,1)}), bf16[8,200,1600]{2,1,0:T(8,128)(2,1)}, u32[]{:S(2)}, u32[]{:S(2)}) %all-to-all-start) | async-done | bytes 5120032 | tf_op jit(solution)/shard_map/all_to_all | solution.py:16
  489.3 7.4 %fusion = bf16[512,1600]{0,1:T(8,128)(2,1)} fusion(bf16[1600,1600]{1,0:T(8,128)(2,1)} %bitcast.9, bf16[512,1600]{0,1:T(8,128)(2,1)} %param.18), kind=kOutput, calls=%fused_computation.3 | convolution fusion | flops 2622259200 | bytes 8396800 | tf_op jit(solution)/shard_map/dot_general | solution.py:61
  (8 shorter events, 0.1 us)
Async XLA Ops:
  7.2 1.4 copy-start
  7.2 58.1 %reduce-scatter.4.cloned.1.call-start = ((), (), s32[]{:S(2)}) async-start(), calls=%async_computation.5 | async-start | bytes 5990400
  14.9 1.4 copy-start.3
  15.0 203.4 %all-reduce.5.cloned.1.call-start = ((), (), s32[]{:S(2)}) async-start(), calls=%async_computation.2 | async-start | bytes 2768896 | tf_op jit(solution)/shard_map/psum | solution.py:38
  66.9 1.1 copy-start.2
  68.0 150.4 %copy-start.4 = (f32[1600,32]{0,1:T(8,128)S(1)}, f32[1600,32]{0,1:T(8,128)}, u32[]{:S(2)}) copy-start(f32[1600,32]{0,1:T(8,128)} %param.17) | copy-start | bytes 614404
  69.2 247.4 %all-reduce.7.cloned.1.call-start = ((), (), s32[]{:S(2)}) async-start(), calls=%async_computation.3 | async-start | bytes 425984 | tf_op jit(solution)/shard_map/psum | solution.py:55
  218.4 3.0 copy-start.1
  256.0 158.7 %all-reduce.9.cloned.1.call-start = ((), (), s32[]{:S(2)}) async-start(), calls=%async_computation.4 | async-start | bytes 425984 | tf_op jit(solution)/shard_map/psum | solution.py:55
  422.3 6.0 %copy-start.5 = (f32[1600]{0:T(1024)S(1)}, f32[1600]{0:T(1024)}, u32[]{:S(2)}) copy-start(f32[1600]{0:T(1024)} %param.16) | copy-start | bytes 19204
  422.3 66.9 %all-to-all-start = ((bf16[8,200,1600]{2,1,0:T(8,128)(2,1)}), bf16[8,200,1600]{2,1,0:T(8,128)(2,1)}, u32[]{:S(2)}, u32[]{:S(2)}) async-start(bf16[8,200,1600]{2,1,0:T(8,128)(2,1)} %stack.2), calls=%async_computation | async-start | bytes 10649600 | tf_op jit(solution)/shard_map/all_to_all | solution.py:16
Sparse Core Ops, SparseCore 0:
  15.1 50.1 reduce-scatter.3
  69.3 148.9 all-reduce.4
  256.1 60.4 all-reduce.6
  349.8 64.7 all-reduce.8
